TPU v7x, 512 devices: a whole 4x8x8 slice. The times are simulated.
512 devices in a mesh: section: 4 (over x_lo, core), batch: 128 (over z, y, x_hi).
Axes of the slice: x: 4 (x_hi: 2, x_lo: 2; x = x_hi * 2 + x_lo), y: 8, z: 8, core: 2. Of those that a mesh axis runs over, the one named last changes fastest.
Arguments:
- latents: bfloat16 [4096, 512], P('batch'), may hold values from -6 to 6
- token_slot: int32 [4096], P('batch'), may hold values from 0 to 4095, as said below
- cache_keys: bfloat16 [4096, 128, 512], P('batch', None, 'section'), may hold values from -320 to 320
- cache_values: bfloat16 [4096, 128, 512], P('batch', None, 'section'), may hold values from -6 to 6
- up_state: bfloat16 [4096, 512], P('batch'), may hold values from -6 to 6
- conv_state: bfloat16 [4096, 512], P('batch'), may hold values from -1 to 3
- cache_slot: int32 [4096], P('batch'), may hold values from 0 to 4095, as said below
- positions: int32 [4096], P('batch'), may hold values from 0 to 512
- up_kernel: float32 [4, 512], replicated, may hold values from -4 to 4
- norm_gain_one: float32 [512], replicated, may hold values from 0.1 to 1.9
- qkv_weight: bfloat16 [3, 512, 512], P(None, None, 'section'), may hold values from -0.25 to 0.25
- out_weight: bfloat16 [512, 512], P('section'), may hold values from -0.25 to 0.25
- scale_attention: float32 [512], replicated, may hold values from 0.1 to 1.9
- norm_gain_two: float32 [512], replicated, may hold values from 0.1 to 1.9
- in_weight: bfloat16 [512, 2048], P(None, 'section'), may hold values from -0.25 to 0.25
- down_weight: bfloat16 [2048, 512], P('section'), may hold values from -0.125 to 0.125
- scale_feedforward: float32 [512], replicated, may hold values from 0.1 to 1.9
- conv_weight: bfloat16 [16, 256, 512], P(None, 'section'), may hold values from -0.1875 to 0.1875
- conv_bias: float32 [256], P('section'), may hold values from -3 to 3
Outputs:
- audio_out: float32 [256, 65536], P('section', 'batch')
- new_keys: bfloat16 [4096, 128, 512], P('batch', None, 'section')
- new_values: bfloat16 [4096, 128, 512], P('batch', None, 'section')
- new_up_state: bfloat16 [4096, 512], P('batch')
- new_conv_state: bfloat16 [4096, 512], P('batch')
Inputs may be any that keep to these rules, and one draw needn't show every extreme that they name: `token_slot`: every slot receives exactly one token row. The 32 rows of one transformer owner go in groups of exactly 2 rows to 16 different decoder owners; the decoder owner of slot n is n // 32. `cache_slot`: A permutation of the slots. Each batch index keeps all but 2 * 1 of its streams and hands exactly 1 to the index one higher and 1 to the index one lower, cyclically.
All inputs are finite; a program needn't handle non-finite values.
Results may differ from a plain program's by a relative error of at most 0.017.
Values may be sent and summed in bfloat16 or wider, within the bound.
No kernel may reach another device: no remote copies, remote signals or barrier semaphores. Data moves between devices by JAX's collectives and lax.ppermute only.
A program may use at most 64 MiB of HBM per device.

v0:
```python
import jax
import jax.numpy as jnp
from jax import lax
from jax.sharding import PartitionSpec as P

HEAD_DIM = 64
MOVE = 1
EPSILON = 1e-05
MAX_PERIOD = 10000.0


def for_sending(array):

    def short(part):
        return part.astype(jnp.bfloat16) if part.dtype == jnp.float32 else part

    return jax.tree.map(short, array)


def passed_along(block, axis, distance):
    devices = range(lax.axis_size(axis))
    route = [((i - distance) % len(devices), i) for i in devices]
    return lax.ppermute(block, axis, route)


def layer_norm(hidden, weight_gain):
    average = jnp.mean(hidden, axis=-1, keepdims=True)
    centred = hidden - average
    variance = jnp.mean(centred * centred, axis=-1, keepdims=True)
    return centred * lax.rsqrt(variance + EPSILON) * weight_gain


def rotate(features, times, head_width):
    streams = features.shape[0]
    half = head_width // 2
    freqs = MAX_PERIOD ** (-2.0 * jnp.arange(half, dtype=jnp.float32) / head_width)
    angle = times.astype(jnp.float32)[:, :, None] * freqs[None, None, :]
    cosine = jnp.cos(angle)[:, :, None, :]
    sine = jnp.sin(angle)[:, :, None, :]
    paired = features.reshape(streams, 2, -1, half, 2)
    first = paired[..., 0]
    second = paired[..., 1]
    turned = jnp.stack([first * cosine - second * sine, first * sine + second * cosine], axis=-1)
    return turned.reshape(features.shape)


def attend(
    queries, fresh_keys, fresh_values, old_keys, old_values, starts, local_heads, head_width
):
    streams = old_keys.shape[0]
    window = old_keys.shape[1]
    query_heads = queries.reshape(streams, 2, local_heads, head_width)
    cache_heads = old_keys.reshape(streams, window, local_heads, head_width)
    fresh_heads = fresh_keys.reshape(streams, 2, local_heads, head_width)
    score_scale = head_width ** (-0.5)
    cache_scores = (
        jnp.einsum("sfhe,swhe->shfw", query_heads, cache_heads, preferred_element_type=jnp.float32)
        * score_scale
    )
    fresh_scores = (
        jnp.einsum("sfhe,sghe->shfg", query_heads, fresh_heads, preferred_element_type=jnp.float32)
        * score_scale
    )
    cycle_slots = jnp.arange(window, dtype=jnp.int32)
    held_time = starts[:, None] - window + jnp.mod(cycle_slots[None, :] - starts[:, None], window)
    query_times = starts[:, None] + jnp.arange(2, dtype=jnp.int32)[None, :]
    cache_ok = (held_time[:, None, :] >= 0) & (
        held_time[:, None, :] > query_times[:, :, None] - window
    )
    frame_ids = jnp.arange(2, dtype=jnp.int32)
    fresh_ok = frame_ids[None, :] <= frame_ids[:, None]
    allowed = jnp.concatenate(
        [
            jnp.broadcast_to(cache_ok[:, None], (streams, local_heads, 2, window)),
            jnp.broadcast_to(fresh_ok, (streams, local_heads, 2, 2)),
        ],
        axis=-1,
    )
    scores = jnp.concatenate([cache_scores, fresh_scores], axis=-1)
    scores = jnp.where(allowed, scores, -jnp.inf)
    score_max = jnp.max(scores, axis=-1, keepdims=True)
    weights = jnp.where(allowed, jnp.exp(scores - score_max), 0.0)
    denominator = jnp.sum(weights, axis=-1, keepdims=True)
    rounded = weights.astype(jnp.bfloat16)
    value_heads = old_values.reshape(streams, window, local_heads, head_width)
    fresh_value_heads = fresh_values.reshape(streams, 2, local_heads, head_width)
    attended = jnp.einsum(
        "shfw,swhe->sfhe", rounded[..., :window], value_heads, preferred_element_type=jnp.float32
    )
    attended = attended + jnp.einsum(
        "shfg,sghe->sfhe",
        rounded[..., window:],
        fresh_value_heads,
        preferred_element_type=jnp.float32,
    )
    attended = attended / jnp.transpose(denominator, (0, 2, 1, 3))
    return attended.astype(jnp.bfloat16).reshape(streams, 2, local_heads * head_width)


def pack_side(direction_owner, leaving, dest_owner, slot_ids, outgoing):
    chosen = leaving & (dest_owner == direction_owner)
    before = chosen[None, :] & (slot_ids[None, :] < slot_ids[:, None])
    box_place = jnp.where(chosen, jnp.sum(before.astype(jnp.int32), axis=1), MOVE)
    return tuple(
        (
            jnp.zeros((MOVE,) + source_array.shape[1:], source_array.dtype)
            .at[box_place]
            .set(source_array, mode="drop")
            for source_array in outgoing
        )
    )


def local(
    latents,
    token_slot,
    cache_keys,
    cache_values,
    up_state,
    conv_state,
    cache_slot,
    positions,
    up_kernel,
    norm_gain_one,
    qkv_weight,
    out_weight,
    scale_attention,
    norm_gain_two,
    in_weight,
    down_weight,
    scale_feedforward,
    conv_weight,
    conv_bias,
):
    owners = lax.axis_size("batch")
    own_index = lax.axis_index("batch")
    streams = latents.shape[0]
    model_width = latents.shape[1]
    window = cache_keys.shape[1]
    head_share = cache_keys.shape[2]
    capacity = max(2, streams // owners)
    slot_ids = jnp.arange(streams, dtype=jnp.int32)
    target = token_slot // streams
    landing = token_slot % streams
    same_before = (target[None, :] == target[:, None]) & (slot_ids[None, :] < slot_ids[:, None])
    arrival_rank = jnp.sum(same_before.astype(jnp.int32), axis=1)
    send_rows = (
        jnp.zeros((owners, capacity, model_width), jnp.bfloat16)
        .at[target, arrival_rank]
        .set(latents)
    )
    send_codes = (
        jnp.zeros((owners, capacity), jnp.bfloat16)
        .at[target, arrival_rank]
        .set((landing + 1).astype(jnp.bfloat16))
    )
    got_rows, got_codes = (
        lax.all_to_all(send_rows, "batch", split_axis=0, concat_axis=0, tiled=True),
        lax.all_to_all(send_codes, "batch", split_axis=0, concat_axis=0, tiled=True),
    )
    selector = got_codes.reshape(-1).astype(jnp.int32)[None, :] - 1 == slot_ids[:, None]
    arrived = jnp.dot(
        selector.astype(jnp.bfloat16),
        got_rows.reshape(owners * capacity, model_width),
        preferred_element_type=jnp.float32,
    ).astype(jnp.bfloat16)
    dest_owner = cache_slot // streams
    dest_local = cache_slot % streams
    leaving = dest_owner != own_index
    stay_codes = jnp.where(leaving, 0, dest_local + 1).astype(jnp.bfloat16)
    code_values = (dest_local + 1).astype(jnp.bfloat16)
    outgoing = (cache_keys, cache_values, up_state, conv_state, code_values)
    right_owner = jnp.mod(own_index + 1, owners)
    left_owner = jnp.mod(own_index + owners - 1, owners)
    right_parts = pack_side(right_owner, leaving, dest_owner, slot_ids, outgoing)
    left_parts = pack_side(left_owner, leaving, dest_owner, slot_ids, outgoing)
    from_left = jax.tree.map(
        lambda part, own: part.astype(own.dtype),
        passed_along(for_sending(right_parts), "batch", 1),
        right_parts,
    )
    from_right = jax.tree.map(
        lambda part, own: part.astype(own.dtype),
        passed_along(for_sending(left_parts), "batch", -1),
        left_parts,
    )
    incoming = tuple(
        (
            jnp.concatenate([lower_part, upper_part], axis=0)
            for lower_part, upper_part in zip(from_left, from_right)
        )
    )
    candidate = tuple(
        (
            jnp.concatenate([own_array, extra_array], axis=0)
            for own_array, extra_array in zip(
                (cache_keys, cache_values, up_state, conv_state, stay_codes), incoming
            )
        )
    )
    candidate_codes = candidate[4].astype(jnp.int32) - 1
    matches = candidate_codes[None, :] == slot_ids[:, None]
    picked = jnp.sum(
        jnp.where(matches, jnp.arange(candidate_codes.shape[0], dtype=jnp.int32)[None, :], 0),
        axis=1,
    )
    keys_old = jnp.take(candidate[0], picked, axis=0)
    values_old = jnp.take(candidate[1], picked, axis=0)
    up_prev = jnp.take(candidate[2], picked, axis=0)
    conv_prev = jnp.take(candidate[3], picked, axis=0)
    latent_f = arrived.astype(jnp.float32)
    prior_f = up_prev.astype(jnp.float32)
    residual_zero = jnp.stack(
        [
            latent_f * up_kernel[0] + prior_f * up_kernel[2],
            latent_f * up_kernel[1] + prior_f * up_kernel[3],
        ],
        axis=1,
    )
    normed_one = layer_norm(residual_zero, norm_gain_one).astype(jnp.bfloat16)
    projections = jnp.einsum(
        "sfd,kde->ksfe", normed_one, qkv_weight, preferred_element_type=jnp.float32
    )
    times = positions[:, None] + jnp.arange(2, dtype=jnp.int32)[None, :]
    queries = rotate(projections[0], times, HEAD_DIM).astype(jnp.bfloat16)
    fresh_keys = rotate(projections[1], times, HEAD_DIM).astype(jnp.bfloat16)
    fresh_values = projections[2].astype(jnp.bfloat16)
    attended = attend(
        queries,
        fresh_keys,
        fresh_values,
        keys_old,
        values_old,
        positions,
        head_share // HEAD_DIM,
        HEAD_DIM,
    )
    partial_heads = jnp.dot(
        attended.reshape(2 * streams, head_share), out_weight, preferred_element_type=jnp.float32
    )
    mixing = lax.psum(partial_heads.astype(jnp.bfloat16), "section").astype(jnp.float32)
    residual_one = residual_zero + scale_attention * mixing.reshape(streams, 2, model_width)
    normed_two = (
        layer_norm(residual_one, norm_gain_two)
        .astype(jnp.bfloat16)
        .reshape(2 * streams, model_width)
    )
    inner_units = jax.nn.gelu(
        jnp.dot(normed_two, in_weight, preferred_element_type=jnp.float32), approximate=False
    ).astype(jnp.bfloat16)
    partial_units = jnp.dot(inner_units, down_weight, preferred_element_type=jnp.float32)
    feed_forward = lax.psum(partial_units.astype(jnp.bfloat16), "section").astype(jnp.float32)
    residual_two = residual_one + scale_feedforward * feed_forward.reshape(streams, 2, model_width)
    excited = jax.nn.elu(residual_two).astype(jnp.bfloat16)
    earlier = jnp.stack([conv_prev, excited[:, 0]], axis=1)
    stride = conv_weight.shape[0] // 2
    audio_out = jnp.einsum(
        "sfi,rci->csfr", excited, conv_weight[:stride], preferred_element_type=jnp.float32
    )
    audio_out = audio_out + jnp.einsum(
        "sfi,rci->csfr", earlier, conv_weight[stride:], preferred_element_type=jnp.float32
    )
    audio_out = audio_out + conv_bias[:, None, None, None]
    audio_out = audio_out.reshape(conv_bias.shape[0], streams * 2 * stride)
    slot_first = jnp.mod(positions, window)
    slot_second = jnp.mod(positions + 1, window)
    new_keys = (
        keys_old.at[slot_ids, slot_first]
        .set(fresh_keys[:, 0])
        .at[slot_ids, slot_second]
        .set(fresh_keys[:, 1])
    )
    new_values = (
        values_old.at[slot_ids, slot_first]
        .set(fresh_values[:, 0])
        .at[slot_ids, slot_second]
        .set(fresh_values[:, 1])
    )
    return (audio_out, new_keys, new_values, arrived, excited[:, 1])


def solution(mesh):
    placed = (
        P("batch", None),
        P("batch"),
        P("batch", None, "section"),
        P("batch", None, "section"),
        P("batch", None),
        P("batch", None),
        P("batch"),
        P("batch"),
        P(),
        P(),
        P(None, None, "section"),
        P("section", None),
        P(),
        P(),
        P(None, "section"),
        P("section", None),
        P(),
        P(None, "section", None),
        P("section"),
    )
    return jax.shard_map(
        local,
        mesh=mesh,
        in_specs=placed,
        out_specs=(
            P("section", "batch"),
            P("batch", None, "section"),
            P("batch", None, "section"),
            P("batch", None),
            P("batch", None),
        ),
        check_vma=False,
    )
```

profile of v0, /device:TPU:1, one launch (start us, length us, event | category | flops | bytes accessed | tf_op | source)
XLA Modules:
  0.0 243.5 jit_solution(4903698463168684158)
XLA Ops:
  7.2 0.7 fusion.107
  8.1 2.0 scatter_fusion
  10.2 0.8 copy.94
  10.9 20.8 %all-to-all-start = ((bf16[128,1,2]{2,1,0:T(2,128)(2,1)}), bf16[128,1,2]{2,1,0:T(2,128)(2,1)S(1)}, u32[]{:S(2)}, u32[]{:S(2)}) async-start(bf16[128,1,2]{2,1,0:T(2,128)(2,1)} %copy.94), calls=%async_computation | async-start | bytes 131072 | tf_op jit(solution)/shard_map/all_to_all | solution.py:159
  32.0 0.7 scatter_custom_fusion.3
  32.7 9.0 %collective-permute-start.1 = (bf16[1,512]{1,0:T(2,128)(2,1)S(1)}, bf16[1,512]{1,0:T(2,128)(2,1)S(1)}, u32[]{:S(2)}, u32[]{:S(2)}) collective-permute-start(bf16[1,512]{1,0:T(2,128)(2,1)S(1)} %bitcast.138), channel_id=1, source_target_pairs={{1,0},{2,1},{3,2},{4,3},{5,4},{6,5},{7,6},{8,7},{9,8},{10,9},{11,1... | collective-permute-start | bytes 3080 | tf_op jit(solution)/shard_map/ppermute | solution.py:23
  41.8 0.7 scatter_custom_fusion.2
  42.5 1.9 collective-permute-start
  44.4 1.8 scatter_fusion.3
  46.2 9.1 %collective-permute-start.3 = (bf16[1]{0:T(256)(128)(2,1)}, bf16[1]{0:T(256)(128)(2,1)}, u32[]{:S(2)}, u32[]{:S(2)}) collective-permute-start(bf16[1]{0:T(256)(128)(2,1)} %scatter_fusion.3), channel_id=1, source_target_pairs={{1,0},{2,1},{3,2},{4,3},{5,4},{6,5},{7,6},{8,7},{9,8},{10,9},{11,1... | collective-permute-start | bytes 14 | tf_op jit(solution)/shard_map/ppermute | solution.py:23
  55.3 1.8 scatter_fusion.2
  57.0 1.9 collective-permute-start.2
  59.0 1.7 scatter_fusion.5
  60.7 9.1 %collective-permute-start.5 = (bf16[1,128,128]{2,1,0:T(8,128)(2,1)S(1)}, bf16[1,128,128]{2,1,0:T(8,128)(2,1)S(1)}, u32[]{:S(2)}, u32[]{:S(2)}) collective-permute-start(bf16[1,128,128]{2,1,0:T(8,128)(2,1)S(1)} %bitcast.120), channel_id=1, source_target_pairs={{1,0},{2,1},{3,2},{4,3},{5,4},{6,5},{7,6},{8,7},{9,8},{10,9},{11,1... | collective-permute-start | bytes 98312 | tf_op jit(solution)/shard_map/ppermute | solution.py:23
  70.2 1.7 scatter_fusion.4
  71.9 1.7 scatter_fusion.7
  73.7 1.7 scatter_fusion.6
  75.4 0.7 scatter_custom_fusion.11
  76.1 0.7 scatter_custom_fusion.10
  76.8 0.8 broadcast_in_dim.65
  77.6 4.4 %scatter_fusion.1 = bf16[128,2,512]{2,1,0:T(2,128)(2,1)} fusion(bf16[128,2,512]{2,1,0:T(2,128)(2,1)} %broadcast_in_dim.65, s32[32]{0:T(128)S(1)} %fusion.115, bf16[32,512]{1,0:T(8,128)(2,1)S(1)} %copy-done.10), kind=kCustom, calls=%fused_computation.5 | custom fusion | bytes 98560 | tf_op jit(solution)/shard_map/scatter | solution.py:150
  82.1 0.2 multiply_cosine_fusion
  82.4 1.9 collective-permute-start.9
  84.3 4.9 %collective-permute-start.8 = (bf16[1,512]{1,0:T(2,128)(2,1)S(1)}, bf16[1,512]{1,0:T(2,128)(2,1)S(1)}, u32[]{:S(2)}, u32[]{:S(2)}) collective-permute-start(bf16[1,512]{1,0:T(2,128)(2,1)S(1)} %bitcast.140), channel_id=1, source_target_pairs={{127,0},{0,1},{1,2},{2,3},{3,4},{4,5},{5,6},{6,7},{7,8},{8,9},{9,1... | collective-permute-start | bytes 3080 | tf_op jit(solution)/shard_map/ppermute | solution.py:23
  89.2 1.3 fusion.114
  90.7 7.8 %all-to-all-start.1 = ((bf16[128,2,512]{2,1,0:T(2,128)(2,1)}), bf16[128,2,512]{2,1,0:T(2,128)(2,1)S(1)}, u32[]{:S(2)}, u32[]{:S(2)}) async-start(bf16[128,2,512]{2,1,0:T(2,128)(2,1)} %scatter_fusion.1), calls=%async_computation.1 | async-start | bytes 524288 | tf_op jit(solution)/shard_map/all_to_all | solution.py:158
  98.6 0.2 add_reduce_fusion
  99.0 4.0 %collective-permute-start.4 = (bf16[1,128,128]{2,1,0:T(8,128)(2,1)S(1)}, bf16[1,128,128]{2,1,0:T(8,128)(2,1)S(1)}, u32[]{:S(2)}, u32[]{:S(2)}) collective-permute-start(bf16[1,128,128]{2,1,0:T(8,128)(2,1)S(1)} %bitcast.121), channel_id=1, source_target_pairs={{127,0},{0,1},{1,2},{2,3},{3,4},{4,5},{5,6},{6,7},{7,8},{8,9},{9,1... | collective-permute-start | bytes 98312 | tf_op jit(solution)/shard_map/ppermute | solution.py:23
  103.0 7.0 %collective-permute-start.7 = (bf16[1,128,128]{2,1,0:T(8,128)(2,1)S(1)}, bf16[1,128,128]{2,1,0:T(8,128)(2,1)S(1)}, u32[]{:S(2)}, u32[]{:S(2)}) collective-permute-start(bf16[1,128,128]{2,1,0:T(8,128)(2,1)S(1)} %bitcast.122), channel_id=1, source_target_pairs={{1,0},{2,1},{3,2},{4,3},{5,4},{6,5},{7,6},{8,7},{9,8},{10,9},{11,1... | collective-permute-start | bytes 98312 | tf_op jit(solution)/shard_map/ppermute | solution.py:23
  110.0 0.6 gather_fusion.3
  110.7 2.1 collective-permute-start.6
  112.9 0.6 gather_fusion
  113.5 1.1 pad_maximum_fusion
  114.7 2.9 %gather_fusion.1 = bf16[32,128,128]{2,1,0:T(8,128)(2,1)} fusion(bf16[34,128,128]{2,1,0:T(8,128)(2,1)} %pad_maximum_fusion, s32[1024]{0:T(1024)S(1)} %pad_clamp_fusion), kind=kCustom, calls=%fused_computation.1.clone | custom fusion | bytes 2097280 | tf_op jit(solution)/shard_map/jit(_take)/gather | solution.py:208
  117.6 3.6 %collective-permute-done.6 = bf16[1,128,128]{2,1,0:T(8,128)(2,1)S(1)} collective-permute-done((bf16[1,128,128]{2,1,0:T(8,128)(2,1)S(1)}, bf16[1,128,128]{2,1,0:T(8,128)(2,1)S(1)}, u32[]{:S(2)}, u32[]{:S(2)}) %collective-permute-start.6) | collective-permute-done | bytes 32800 | tf_op jit(solution)/shard_map/ppermute | solution.py:23
  121.3 1.7 gather_fusion.2
  122.9 1.8 broadcast_select_fusion.1
  124.7 1.3 copy.98
  126.0 1.3 copy.95
  128.0 1.2 convolution_bitcast_fusion
  129.6 0.2 pad_maximum_fusion.3
  130.1 0.2 maximum_convert_fusion
  130.4 0.2 convolution_multiply_fusion
  130.6 1.6 convolution_multiply_fusion.1
  132.4 0.4 fusion.151
  132.8 0.2 fusion.79
  133.0 0.6 copy-done.5
  133.6 0.6 fusion.77
  134.6 0.8 convolution_convert_fusion.1
  135.7 44.9 %all-reduce.3.cloned.1.call-done = bf16[64,512]{1,0:T(8,128)(2,1)} async-done(((bf16[64,512]{1,0:T(8,128)(2,1)}), bf16[64,512]{1,0:T(8,128)(2,1)}) %all-reduce.3.cloned.1.call-update) | async-done | bytes 65552 | tf_op jit(solution)/shard_map/psum | solution.py:241
  180.6 1.0 fusion.82
  181.6 1.0 multiply_reduce_fusion
  182.6 1.8 convolution_convert_fusion
  184.4 0.6 copy.111
  185.3 2.1 scatter_fusion.8
  187.4 2.1 scatter_fusion.10
  189.6 2.1 scatter_fusion.9
  191.7 2.1 scatter_fusion.11
  193.9 38.3 %all-reduce.5.cloned.1.call-done = bf16[32,2,512]{2,0,1:T(8,128)(2,1)} async-done(((bf16[32,2,512]{2,0,1:T(8,128)(2,1)}), bf16[32,2,512]{2,0,1:T(8,128)(2,1)}) %all-reduce.5.cloned.1.call-update) | async-done | bytes 65552 | tf_op jit(solution)/shard_map/psum | solution.py:252
  232.3 1.0 fusion.16
  233.3 0.6 slice_bitcast_fusion
  233.9 1.4 fusion.7
  235.4 0.4 fusion.2
  235.9 0.8 copy.115
  (124 shorter events, 4.2 us)
Async XLA Ops:
  7.2 175.4 %copy-start = (bf16[512,512]{1,0:T(8,128)(2,1)S(1)}, bf16[512,512]{1,0:T(8,128)(2,1)}, u32[]{:S(2)}) copy-start(bf16[512,512]{1,0:T(8,128)(2,1)} %param.38) | copy-start | bytes 1572868
  7.2 24.6 %copy-start.19 = (s32[32]{0:T(128)S(1)}, s32[32]{0:T(128)}, u32[]{:S(2)}) copy-start(s32[32]{0:T(128)} %param.29) | copy-start | bytes 388
  7.2 24.8 %copy-start.12 = (bf16[32,512]{1,0:T(8,128)(2,1)S(1)}, bf16[32,512]{1,0:T(8,128)(2,1)}, u32[]{:S(2)}) copy-start(bf16[32,512]{1,0:T(8,128)(2,1)} %param.27) | copy-start | bytes 98308
  10.9 79.8 %all-to-all-start = ((bf16[128,1,2]{2,1,0:T(2,128)(2,1)}), bf16[128,1,2]{2,1,0:T(2,128)(2,1)S(1)}, u32[]{:S(2)}, u32[]{:S(2)}) async-start(bf16[128,1,2]{2,1,0:T(2,128)(2,1)} %copy.94), calls=%async_computation | async-start | bytes 131072 | tf_op jit(solution)/shard_map/all_to_all | solution.py:159
  31.8 27.2 %copy-start.1 = (bf16[32,128,128]{2,1,0:T(8,128)(2,1)S(1)}, bf16[32,128,128]{2,1,0:T(8,128)(2,1)}, u32[]{:S(2)}) copy-start(bf16[32,128,128]{2,1,0:T(8,128)(2,1)} %param.26) | copy-start | bytes 3145732
  32.7 78.0 %collective-permute-start.1 = (bf16[1,512]{1,0:T(2,128)(2,1)S(1)}, bf16[1,512]{1,0:T(2,128)(2,1)S(1)}, u32[]{:S(2)}, u32[]{:S(2)}) collective-permute-start(bf16[1,512]{1,0:T(2,128)(2,1)S(1)} %bitcast.138), channel_id=1, source_target_pairs={{1,0},{2,1},{3,2},{4,3},{5,4},{6,5},{7,6},{8,7},{9,8},{10,9},{11,1... | collective-permute-start | bytes 3080 | tf_op jit(solution)/shard_map/ppermute | solution.py:23
  42.5 70.4 %collective-permute-start = (bf16[1,512]{1,0:T(2,128)(2,1)S(1)}, bf16[1,512]{1,0:T(2,128)(2,1)S(1)}, u32[]{:S(2)}, u32[]{:S(2)}) collective-permute-start(bf16[1,512]{1,0:T(2,128)(2,1)S(1)} %bitcast.139), channel_id=1, source_target_pairs={{127,0},{0,1},{1,2},{2,3},{3,4},{4,5},{5,6},{6,7},{7,8},{8,9},{9,1... | collective-permute-start | bytes 3080 | tf_op jit(solution)/shard_map/ppermute | solution.py:23
  46.2 38.1 %collective-permute-start.3 = (bf16[1]{0:T(256)(128)(2,1)}, bf16[1]{0:T(256)(128)(2,1)}, u32[]{:S(2)}, u32[]{:S(2)}) collective-permute-start(bf16[1]{0:T(256)(128)(2,1)} %scatter_fusion.3), channel_id=1, source_target_pairs={{1,0},{2,1},{3,2},{4,3},{5,4},{6,5},{7,6},{8,7},{9,8},{10,9},{11,1... | collective-permute-start | bytes 14 | tf_op jit(solution)/shard_map/ppermute | solution.py:23
  57.0 25.3 %collective-permute-start.2 = (bf16[1]{0:T(256)(128)(2,1)}, bf16[1]{0:T(256)(128)(2,1)}, u32[]{:S(2)}, u32[]{:S(2)}) collective-permute-start(bf16[1]{0:T(256)(128)(2,1)} %scatter_fusion.2), channel_id=1, source_target_pairs={{127,0},{0,1},{1,2},{2,3},{3,4},{4,5},{5,6},{6,7},{7,8},{8,9},{9,1... | collective-permute-start | bytes 14 | tf_op jit(solution)/shard_map/ppermute | solution.py:23
  59.0 10.8 %copy-start.15 = (s32[32]{0:T(128)S(1)}, s32[32]{0:T(128)}, u32[]{:S(2)}) copy-start(s32[32]{0:T(128)} %param.30) | copy-start | bytes 388
  59.0 11.2 %copy-start.14 = (f32[4,512]{1,0:T(4,128)S(1)}, f32[4,512]{1,0:T(4,128)}, u32[]{:S(2)}) copy-start(f32[4,512]{1,0:T(4,128)} %param.31) | copy-start | bytes 24580
  60.7 52.8 %collective-permute-start.5 = (bf16[1,128,128]{2,1,0:T(8,128)(2,1)S(1)}, bf16[1,128,128]{2,1,0:T(8,128)(2,1)S(1)}, u32[]{:S(2)}, u32[]{:S(2)}) collective-permute-start(bf16[1,128,128]{2,1,0:T(8,128)(2,1)S(1)} %bitcast.120), channel_id=1, source_target_pairs={{1,0},{2,1},{3,2},{4,3},{5,4},{6,5},{7,6},{8,7},{9,8},{10,9},{11,1... | collective-permute-start | bytes 98312 | tf_op jit(solution)/shard_map/ppermute | solution.py:23
  70.2 1.7 copy-start.2
  73.7 1.7 copy-start.11
  73.7 4.0 %copy-start.10 = (bf16[32,512]{1,0:T(8,128)(2,1)S(1)}, bf16[32,512]{1,0:T(8,128)(2,1)}, u32[]{:S(2)}) copy-start(bf16[32,512]{1,0:T(8,128)(2,1)} %param.23) | copy-start | bytes 98308
  82.4 16.6 %collective-permute-start.9 = (bf16[1,512]{1,0:T(2,128)(2,1)S(1)}, bf16[1,512]{1,0:T(2,128)(2,1)S(1)}, u32[]{:S(2)}, u32[]{:S(2)}) collective-permute-start(bf16[1,512]{1,0:T(2,128)(2,1)S(1)} %bitcast.141), channel_id=1, source_target_pairs={{1,0},{2,1},{3,2},{4,3},{5,4},{6,5},{7,6},{8,7},{9,8},{10,9},{11,1... | collective-permute-start | bytes 3080 | tf_op jit(solution)/shard_map/ppermute | solution.py:23
  84.3 18.6 %collective-permute-start.8 = (bf16[1,512]{1,0:T(2,128)(2,1)S(1)}, bf16[1,512]{1,0:T(2,128)(2,1)S(1)}, u32[]{:S(2)}, u32[]{:S(2)}) collective-permute-start(bf16[1,512]{1,0:T(2,128)(2,1)S(1)} %bitcast.140), channel_id=1, source_target_pairs={{127,0},{0,1},{1,2},{2,3},{3,4},{4,5},{5,6},{6,7},{7,8},{8,9},{9,1... | collective-permute-start | bytes 3080 | tf_op jit(solution)/shard_map/ppermute | solution.py:23
  90.7 36.6 %all-to-all-start.1 = ((bf16[128,2,512]{2,1,0:T(2,128)(2,1)}), bf16[128,2,512]{2,1,0:T(2,128)(2,1)S(1)}, u32[]{:S(2)}, u32[]{:S(2)}) async-start(bf16[128,2,512]{2,1,0:T(2,128)(2,1)} %scatter_fusion.1), calls=%async_computation.1 | async-start | bytes 524288 | tf_op jit(solution)/shard_map/all_to_all | solution.py:158
  98.5 82.0 %all-reduce.3.cloned.1.call-start = ((), (), s32[]{:S(2)}) async-start(), calls=%async_computation.2 | async-start | bytes 131072 | tf_op jit(solution)/shard_map/psum | solution.py:241
  99.0 14.5 %collective-permute-start.4 = (bf16[1,128,128]{2,1,0:T(8,128)(2,1)S(1)}, bf16[1,128,128]{2,1,0:T(8,128)(2,1)S(1)}, u32[]{:S(2)}, u32[]{:S(2)}) collective-permute-start(bf16[1,128,128]{2,1,0:T(8,128)(2,1)S(1)} %bitcast.121), channel_id=1, source_target_pairs={{127,0},{0,1},{1,2},{2,3},{3,4},{4,5},{5,6},{6,7},{7,8},{8,9},{9,1... | collective-permute-start | bytes 98312 | tf_op jit(solution)/shard_map/ppermute | solution.py:23
  103.0 14.6 %collective-permute-start.7 = (bf16[1,128,128]{2,1,0:T(8,128)(2,1)S(1)}, bf16[1,128,128]{2,1,0:T(8,128)(2,1)S(1)}, u32[]{:S(2)}, u32[]{:S(2)}) collective-permute-start(bf16[1,128,128]{2,1,0:T(8,128)(2,1)S(1)} %bitcast.122), channel_id=1, source_target_pairs={{1,0},{2,1},{3,2},{4,3},{5,4},{6,5},{7,6},{8,7},{9,8},{10,9},{11,1... | collective-permute-start | bytes 98312 | tf_op jit(solution)/shard_map/ppermute | solution.py:23
  110.7 10.4 %collective-permute-start.6 = (bf16[1,128,128]{2,1,0:T(8,128)(2,1)S(1)}, bf16[1,128,128]{2,1,0:T(8,128)(2,1)S(1)}, u32[]{:S(2)}, u32[]{:S(2)}) collective-permute-start(bf16[1,128,128]{2,1,0:T(8,128)(2,1)S(1)} %bitcast.123), channel_id=1, source_target_pairs={{127,0},{0,1},{1,2},{2,3},{3,4},{4,5},{5,6},{6,7},{7,8},{8,9},{9,1... | collective-permute-start | bytes 98312 | tf_op jit(solution)/shard_map/ppermute | solution.py:23
  127.3 0.7 copy-start.16
  127.6 2.4 copy-start.8
  132.4 1.2 copy-start.5
  132.8 1.8 copy-start.9
  133.6 47.0 %copy-start.13 = (f32[512]{0:T(512)S(1)}, f32[512]{0:T(512)}, u32[]{:S(2)}) copy-start(f32[512]{0:T(512)} %param.35) | copy-start | bytes 6148
  134.3 48.4 %copy-start.20 = (f32[512]{0:T(512)S(1)}, f32[512]{0:T(512)}, u32[]{:S(2)}) copy-start(f32[512]{0:T(512)} %param.36) | copy-start | bytes 6148
  135.4 96.9 %all-reduce.5.cloned.1.call-start = ((), (), s32[]{:S(2)}) async-start(), calls=%async_computation.3 | async-start | bytes 131072 | tf_op jit(solution)/shard_map/psum | solution.py:252
  184.4 9.4 %copy-start.7 = (bf16[64,512]{1,0:T(8,128)(2,1)S(1)}, bf16[64,512]{1,0:T(8,128)(2,1)}, u32[]{:S(2)}) copy-start(bf16[64,512]{1,0:T(8,128)(2,1)} %all-reduce.3.cloned.1.call-done) | copy-start | bytes 196612
  184.4 47.9 %copy-start.17 = (f32[512]{0:T(512)S(1)}, f32[512]{0:T(512)}, u32[]{:S(2)}) copy-start(f32[512]{0:T(512)} %param.39) | copy-start | bytes 6148
  185.3 50.1 %copy-start.18 = (f32[64]{0:T(128)S(1)}, f32[64]{0:T(128)}, u32[]{:S(2)}) copy-start(f32[64]{0:T(128)} %param.41) | copy-start | bytes 772
  191.7 44.0 %copy-start.4 = (bf16[32,128,128]{2,1,0:T(8,128)(2,1)}, bf16[32,128,128]{2,1,0:T(8,128)(2,1)S(1)}, u32[]{:S(2)}) copy-start(bf16[32,128,128]{2,1,0:T(8,128)(2,1)S(1)} %scatter_fusion.9) | copy-start | bytes 3145732
  193.8 41.9 %copy-start.3 = (bf16[32,128,128]{2,1,0:T(8,128)(2,1)}, bf16[32,128,128]{2,1,0:T(8,128)(2,1)S(1)}, u32[]{:S(2)}) copy-start(bf16[32,128,128]{2,1,0:T(8,128)(2,1)S(1)} %scatter_fusion.11) | copy-start | bytes 3145732
  232.3 3.1 %copy-start.6 = (bf16[16,64,512]{2,1,0:T(8,128)(2,1)S(1)}, bf16[16,64,512]{2,1,0:T(8,128)(2,1)}, u32[]{:S(2)}) copy-start(bf16[16,64,512]{2,1,0:T(8,128)(2,1)} %param.40) | copy-start | bytes 3145732
Sparse Core Ops, SparseCore 0:
  135.5 45.0 all-reduce.2
  185.2 47.0 all-reduce.4
where the time goes:
time: 244 us
  waiting for transfers between devices  86.8 us (36%)
  starting transfers between devices  79.6 us (33%)
  local copies, waits for them, and re-layouts  42.6 us (17%)
  between operations  15 us (6%)
  other arithmetic  11.2 us (5%)
  matrix products  8.35 us (3%)
    ppermute x10, starting transfers between devices, passed_along(): return lax.ppermute(block, axis, route)  50.8 us
    psum x1, waiting for transfers between devices, local(): lax.psum(partial_heads.astype(jnp.bfloat16), 'section').astype(jnp.float32)  44.9 us
    psum x1, waiting for transfers between devices, local(): lax.psum(partial_units.astype(jnp.bfloat16), 'section').astype(jnp.float32)  38.3 us
    all_to_all x1, starting transfers between devices, local(): lax.all_to_all(send_codes, 'batch', split_axis=0, concat_axis=0, tiled=True)  20.8 us
    scatter x10, local copies, waits for them, and re-layouts, pack_side(): return tuple((jnp.zeros((MOVE,) + source_array.shape[1:], source_array.dt...  13.1 us
    all_to_all x1, starting transfers between devices, local(): lax.all_to_all(send_rows, 'batch', split_axis=0, concat_axis=0, tiled=True)  7.84 us
  transfers between devices with their start and end apart: 14, of which 3 were waited for; matrix products, arithmetic and copies ran while one was open for 17% of the time, Pallas kernels for 0%

commit v1 on v0

--- a/solution.py
+++ b/solution.py
@@ -249,7 +249,9 @@
         jnp.dot(normed_two, in_weight, preferred_element_type=jnp.float32), approximate=False
     ).astype(jnp.bfloat16)
     partial_units = jnp.dot(inner_units, down_weight, preferred_element_type=jnp.float32)
-    feed_forward = lax.psum(partial_units.astype(jnp.bfloat16), "section").astype(jnp.float32)
+    feed_forward = jnp.sum(
+        lax.all_gather(partial_units.astype(jnp.bfloat16), "section"), axis=0
+    ).astype(jnp.float32)
     residual_two = residual_one + scale_feedforward * feed_forward.reshape(streams, 2, model_width)
     excited = jax.nn.elu(residual_two).astype(jnp.bfloat16)
     earlier = jnp.stack([conv_prev, excited[:, 0]], axis=1)

time: 244 us -> 201 us (0.82)
  waiting for transfers between devices: 86.8 us -> 39.8 us
  blocking collectives: 0 us -> 5.86 us
    psum x1 -> x0, waiting for transfers between devices: 38.3 us -> none  [local(): lax.psum(partial_units.astype(jnp.bfloat16), 'section').astype(jnp.float32)]
    psum x1, waiting for transfers between devices: 44.9 us -> 36.2 us  [local(): lax.psum(partial_heads.astype(jnp.bfloat16), 'section').astype(jnp.float32)]
    all_gather x0 -> x1, blocking collectives: none -> 5.86 us  [local(): lax.all_gather(partial_units.astype(jnp.bfloat16), 'section')]
  transfers between devices with their start and end apart: 14 -> 13, of which waited for: 3 -> 2; matrix products, arithmetic and copies ran while one was open for 17% -> 21% of each run, Pallas kernels for 0% -> 0%
where the time goes in v1:
time: 201 us; the launch traced here: 200 us
  starting transfers between devices  79.5 us (40%)
  local copies, waits for them, and re-layouts  42.3 us (21%)
  waiting for transfers between devices  39.8 us (20%)
  between operations  15 us (7%)
  other arithmetic  10.3 us (5%)
  matrix products  7.34 us (4%)
  blocking collectives  5.86 us (3%)
    ppermute x10, starting transfers between devices, passed_along(): return lax.ppermute(block, axis, route)  50.8 us
    psum x1, waiting for transfers between devices, local(): lax.psum(partial_heads.astype(jnp.bfloat16), 'section').astype(jnp.float32)  36.2 us
    all_to_all x1, starting transfers between devices, local(): lax.all_to_all(send_codes, 'batch', split_axis=0, concat_axis=0, tiled=True)  20.8 us
    scatter x10, local copies, waits for them, and re-layouts, pack_side(): return tuple((jnp.zeros((MOVE,) + source_array.shape[1:], source_array.dt...  13.1 us
    all_to_all x1, starting transfers between devices, local(): lax.all_to_all(send_rows, 'batch', split_axis=0, concat_axis=0, tiled=True)  7.84 us
    all_gather x1, blocking collectives, local(): lax.all_gather(partial_units.astype(jnp.bfloat16), 'section')  5.86 us
    scatter x1, local copies, waits for them, and re-layouts, local(): send_rows = jnp.zeros((owners, capacity, model_width), jnp.bfloat16).at[t...  4.44 us
    scatter x2, local copies, waits for them, and re-layouts, local(): new_keys = keys_old.at[slot_ids, slot_first].set(fresh_keys[:, 0]).at[slo...  4.27 us
  transfers between devices with their start and end apart: 13, of which 2 were waited for; matrix products, arithmetic and copies ran while one was open for 21% of the time, Pallas kernels for 0%

profile of v1, /device:TPU:1, one launch (start us, length us, event | category | flops | bytes accessed | tf_op | source)
XLA Modules:
  0.0 200.1 jit_solution(1457648365820301183)
XLA Ops:
  7.2 0.7 fusion.107
  7.9 0.2 convert_reduce_fusion.2
  8.1 2.0 %scatter_fusion = bf16[128,2]{0,1:T(2,128)(2,1)S(1)} fusion(bf16[128,2]{0,1:T(2,128)(2,1)S(1)} %broadcast_in_dim.63, s32[32]{0:T(128)S(1)} %fusion.115, bf16[32]{0:T(256)(128)(2,1)S(1)} %get-tuple-element.62), kind=kCustom, calls=%fused_computation.4 | custom fusion | bytes 448 | tf_op jit(solution)/shard_map/scatter | solution.py:155
  10.2 0.8 copy.94
  10.9 20.8 %all-to-all-start = ((bf16[128,1,2]{2,1,0:T(2,128)(2,1)}), bf16[128,1,2]{2,1,0:T(2,128)(2,1)S(1)}, u32[]{:S(2)}, u32[]{:S(2)}) async-start(bf16[128,1,2]{2,1,0:T(2,128)(2,1)} %copy.94), calls=%async_computation | async-start | bytes 131072 | tf_op jit(solution)/shard_map/all_to_all | solution.py:159
  32.0 0.7 scatter_custom_fusion.3
  32.7 9.0 %collective-permute-start.1 = (bf16[1,512]{1,0:T(2,128)(2,1)S(1)}, bf16[1,512]{1,0:T(2,128)(2,1)S(1)}, u32[]{:S(2)}, u32[]{:S(2)}) collective-permute-start(bf16[1,512]{1,0:T(2,128)(2,1)S(1)} %bitcast.140), channel_id=1, source_target_pairs={{1,0},{2,1},{3,2},{4,3},{5,4},{6,5},{7,6},{8,7},{9,8},{10,9},{11,1... | collective-permute-start | bytes 3080 | tf_op jit(solution)/shard_map/ppermute | solution.py:23
  41.8 0.7 scatter_custom_fusion.2
  42.5 1.9 collective-permute-start
  44.4 1.8 scatter_fusion.3
  46.2 9.1 %collective-permute-start.3 = (bf16[1]{0:T(256)(128)(2,1)}, bf16[1]{0:T(256)(128)(2,1)}, u32[]{:S(2)}, u32[]{:S(2)}) collective-permute-start(bf16[1]{0:T(256)(128)(2,1)} %scatter_fusion.3), channel_id=1, source_target_pairs={{1,0},{2,1},{3,2},{4,3},{5,4},{6,5},{7,6},{8,7},{9,8},{10,9},{11,1... | collective-permute-start | bytes 14 | tf_op jit(solution)/shard_map/ppermute | solution.py:23
  55.3 1.8 scatter_fusion.2
  57.0 1.9 collective-permute-start.2
  59.0 1.7 scatter_fusion.5
  60.7 9.1 %collective-permute-start.5 = (bf16[1,128,128]{2,1,0:T(8,128)(2,1)S(1)}, bf16[1,128,128]{2,1,0:T(8,128)(2,1)S(1)}, u32[]{:S(2)}, u32[]{:S(2)}) collective-permute-start(bf16[1,128,128]{2,1,0:T(8,128)(2,1)S(1)} %bitcast.121), channel_id=1, source_target_pairs={{1,0},{2,1},{3,2},{4,3},{5,4},{6,5},{7,6},{8,7},{9,8},{10,9},{11,1... | collective-permute-start | bytes 98312 | tf_op jit(solution)/shard_map/ppermute | solution.py:23
  70.2 1.7 scatter_fusion.4
  71.9 1.7 scatter_fusion.7
  73.7 1.7 scatter_fusion.6
  75.4 0.7 scatter_custom_fusion.11
  76.1 0.7 scatter_custom_fusion.10
  76.8 0.8 broadcast_in_dim.65
  77.6 4.4 %scatter_fusion.1 = bf16[128,2,512]{2,1,0:T(2,128)(2,1)} fusion(bf16[128,2,512]{2,1,0:T(2,128)(2,1)} %broadcast_in_dim.65, s32[32]{0:T(128)S(1)} %fusion.115, bf16[32,512]{1,0:T(8,128)(2,1)S(1)} %copy-done.10), kind=kCustom, calls=%fused_computation.5 | custom fusion | bytes 98560 | tf_op jit(solution)/shard_map/scatter | solution.py:150
  82.1 0.2 multiply_cosine_fusion
  82.4 1.9 collective-permute-start.9
  84.3 4.9 %collective-permute-start.8 = (bf16[1,512]{1,0:T(2,128)(2,1)S(1)}, bf16[1,512]{1,0:T(2,128)(2,1)S(1)}, u32[]{:S(2)}, u32[]{:S(2)}) collective-permute-start(bf16[1,512]{1,0:T(2,128)(2,1)S(1)} %bitcast.142), channel_id=1, source_target_pairs={{127,0},{0,1},{1,2},{2,3},{3,4},{4,5},{5,6},{6,7},{7,8},{8,9},{9,1... | collective-permute-start | bytes 3080 | tf_op jit(solution)/shard_map/ppermute | solution.py:23
  89.2 1.3 fusion.114
  90.7 7.8 %all-to-all-start.1 = ((bf16[128,2,512]{2,1,0:T(2,128)(2,1)}), bf16[128,2,512]{2,1,0:T(2,128)(2,1)S(1)}, u32[]{:S(2)}, u32[]{:S(2)}) async-start(bf16[128,2,512]{2,1,0:T(2,128)(2,1)} %scatter_fusion.1), calls=%async_computation.1 | async-start | bytes 524288 | tf_op jit(solution)/shard_map/all_to_all | solution.py:158
  98.6 0.2 add_reduce_fusion
  99.0 4.0 %collective-permute-start.4 = (bf16[1,128,128]{2,1,0:T(8,128)(2,1)S(1)}, bf16[1,128,128]{2,1,0:T(8,128)(2,1)S(1)}, u32[]{:S(2)}, u32[]{:S(2)}) collective-permute-start(bf16[1,128,128]{2,1,0:T(8,128)(2,1)S(1)} %bitcast.122), channel_id=1, source_target_pairs={{127,0},{0,1},{1,2},{2,3},{3,4},{4,5},{5,6},{6,7},{7,8},{8,9},{9,1... | collective-permute-start | bytes 98312 | tf_op jit(solution)/shard_map/ppermute | solution.py:23
  103.0 7.0 %collective-permute-start.7 = (bf16[1,128,128]{2,1,0:T(8,128)(2,1)S(1)}, bf16[1,128,128]{2,1,0:T(8,128)(2,1)S(1)}, u32[]{:S(2)}, u32[]{:S(2)}) collective-permute-start(bf16[1,128,128]{2,1,0:T(8,128)(2,1)S(1)} %bitcast.123), channel_id=1, source_target_pairs={{1,0},{2,1},{3,2},{4,3},{5,4},{6,5},{7,6},{8,7},{9,8},{10,9},{11,1... | collective-permute-start | bytes 98312 | tf_op jit(solution)/shard_map/ppermute | solution.py:23
  110.0 0.6 gather_fusion.3
  110.7 2.1 %collective-permute-start.6 = (bf16[1,128,128]{2,1,0:T(8,128)(2,1)S(1)}, bf16[1,128,128]{2,1,0:T(8,128)(2,1)S(1)}, u32[]{:S(2)}, u32[]{:S(2)}) collective-permute-start(bf16[1,128,128]{2,1,0:T(8,128)(2,1)S(1)} %bitcast.124), channel_id=1, source_target_pairs={{127,0},{0,1},{1,2},{2,3},{3,4},{4,5},{5,6},{6,7},{7,8},{8,9},{9,1... | collective-permute-start | bytes 98312 | tf_op jit(solution)/shard_map/ppermute | solution.py:23
  112.9 0.6 gather_fusion
  113.5 1.1 pad_maximum_fusion
  114.7 2.9 %gather_fusion.1 = bf16[32,128,128]{2,1,0:T(8,128)(2,1)} fusion(bf16[34,128,128]{2,1,0:T(8,128)(2,1)} %pad_maximum_fusion, s32[1024]{0:T(1024)S(1)} %pad_clamp_fusion), kind=kCustom, calls=%fused_computation.1.clone | custom fusion | bytes 2097280 | tf_op jit(solution)/shard_map/jit(_take)/gather | solution.py:208
  117.6 3.6 %collective-permute-done.6 = bf16[1,128,128]{2,1,0:T(8,128)(2,1)S(1)} collective-permute-done((bf16[1,128,128]{2,1,0:T(8,128)(2,1)S(1)}, bf16[1,128,128]{2,1,0:T(8,128)(2,1)S(1)}, u32[]{:S(2)}, u32[]{:S(2)}) %collective-permute-start.6) | collective-permute-done | bytes 32800 | tf_op jit(solution)/shard_map/ppermute | solution.py:23
  121.3 1.7 gather_fusion.2
  122.9 1.8 broadcast_select_fusion.1
  124.7 1.3 copy.98
  126.0 1.3 copy.95
  128.0 1.2 convolution_bitcast_fusion
  129.6 0.2 pad_maximum_fusion.3
  130.2 0.2 maximum_convert_fusion
  130.4 0.2 convolution_multiply_fusion
  130.7 1.6 convolution_multiply_fusion.1
  132.4 0.4 fusion.151
  132.9 0.2 fusion.79
  133.1 0.6 copy-done.5
  133.6 0.6 fusion.77
  134.6 0.8 convolution_convert_fusion.1
  135.8 2.1 %scatter_fusion.8 = bf16[32,128,128]{2,1,0:T(8,128)(2,1)S(1)} fusion(bf16[32,128,128]{2,1,0:T(8,128)(2,1)S(1)} %get-tuple-element.57, s32[32]{0:T(128)S(1)} %get-tuple-element.55, bf16[32,128]{1,0:T(8,128)(2,1)S(1)} %copy.113), kind=kCustom, calls=%fused_computation.16 | custom fusion | bytes 24832 | tf_op jit(solution)/shard_map/scatter | solution.py:271
  138.0 2.1 %scatter_fusion.10 = bf16[32,128,128]{2,1,0:T(8,128)(2,1)S(1)} fusion(bf16[32,128,128]{2,1,0:T(8,128)(2,1)S(1)} %get-tuple-element.56, s32[32]{0:T(128)S(1)} %get-tuple-element.55, bf16[32,128]{1,0:T(8,128)(2,1)S(1)} %get-tuple-element.47), kind=kCustom, calls=%fused_computation.18 | custom fusion | bytes 24832 | tf_op jit(solution)/shard_map/scatter | solution.py:277
  140.1 2.1 %scatter_fusion.9 = bf16[32,128,128]{2,1,0:T(8,128)(2,1)S(1)} fusion(bf16[32,128,128]{2,1,0:T(8,128)(2,1)S(1)} %scatter_fusion.8, s32[32]{0:T(128)S(1)} %get-tuple-element.54, bf16[32,128]{1,0:T(8,128)(2,1)S(1)} %copy.114), kind=kCustom, calls=%fused_computation.17 | custom fusion | bytes 24832 | tf_op jit(solution)/shard_map/scatter | solution.py:273
  142.3 2.1 %scatter_fusion.11 = bf16[32,128,128]{2,1,0:T(8,128)(2,1)S(1)} fusion(bf16[32,128,128]{2,1,0:T(8,128)(2,1)S(1)} %scatter_fusion.10, s32[32]{0:T(128)S(1)} %get-tuple-element.54, bf16[32,128]{1,0:T(8,128)(2,1)S(1)} %get-tuple-element.46), kind=kCustom, calls=%fused_computation.19 | custom fusion | bytes 24832 | tf_op jit(solution)/shard_map/scatter | solution.py:279
  144.4 36.2 %all-reduce.2.cloned.1.call-done = bf16[64,512]{1,0:T(8,128)(2,1)} async-done(((bf16[64,512]{1,0:T(8,128)(2,1)}), bf16[64,512]{1,0:T(8,128)(2,1)}) %all-reduce.2.cloned.1.call-update) | async-done | bytes 65552 | tf_op jit(solution)/shard_map/psum | solution.py:241
  180.6 1.0 fusion.82
  181.6 1.0 multiply_reduce_fusion
  182.7 1.8 convolution_convert_fusion
  184.5 5.9 %all-gather = bf16[256,512]{1,0:T(8,128)(2,1)S(1)} all-gather(bf16[64,512]{1,0:T(8,128)(2,1)S(1)} %convolution_convert_fusion), channel_id=2, replica_groups=mesh['section'=4,'batch'=128] {'section'}, dimensions={0}, use_global_device_ids=true | all-gather | bytes 327680 | tf_op jit(solution)/shard_map/all_gather | solution.py:253
  190.7 0.6 slice_bitcast_fusion
  191.3 0.3 copy-done.6
  191.6 0.4 fusion.7
  192.0 0.4 fusion.2
  192.5 0.8 copy.115
  (122 shorter events, 4.1 us)
Async XLA Ops:
  7.2 175.5 %copy-start = (bf16[512,512]{1,0:T(8,128)(2,1)S(1)}, bf16[512,512]{1,0:T(8,128)(2,1)}, u32[]{:S(2)}) copy-start(bf16[512,512]{1,0:T(8,128)(2,1)} %param.38) | copy-start | bytes 1572868
  7.2 24.6 %copy-start.19 = (s32[32]{0:T(128)S(1)}, s32[32]{0:T(128)}, u32[]{:S(2)}) copy-start(s32[32]{0:T(128)} %param.29) | copy-start | bytes 388
  7.2 24.8 %copy-start.12 = (bf16[32,512]{1,0:T(8,128)(2,1)S(1)}, bf16[32,512]{1,0:T(8,128)(2,1)}, u32[]{:S(2)}) copy-start(bf16[32,512]{1,0:T(8,128)(2,1)} %param.27) | copy-start | bytes 98308
  10.9 79.8 %all-to-all-start = ((bf16[128,1,2]{2,1,0:T(2,128)(2,1)}), bf16[128,1,2]{2,1,0:T(2,128)(2,1)S(1)}, u32[]{:S(2)}, u32[]{:S(2)}) async-start(bf16[128,1,2]{2,1,0:T(2,128)(2,1)} %copy.94), calls=%async_computation | async-start | bytes 131072 | tf_op jit(solution)/shard_map/all_to_all | solution.py:159
  31.8 27.2 %copy-start.1 = (bf16[32,128,128]{2,1,0:T(8,128)(2,1)S(1)}, bf16[32,128,128]{2,1,0:T(8,128)(2,1)}, u32[]{:S(2)}) copy-start(bf16[32,128,128]{2,1,0:T(8,128)(2,1)} %param.26) | copy-start | bytes 3145732
  32.7 78.1 %collective-permute-start.1 = (bf16[1,512]{1,0:T(2,128)(2,1)S(1)}, bf16[1,512]{1,0:T(2,128)(2,1)S(1)}, u32[]{:S(2)}, u32[]{:S(2)}) collective-permute-start(bf16[1,512]{1,0:T(2,128)(2,1)S(1)} %bitcast.140), channel_id=1, source_target_pairs={{1,0},{2,1},{3,2},{4,3},{5,4},{6,5},{7,6},{8,7},{9,8},{10,9},{11,1... | collective-permute-start | bytes 3080 | tf_op jit(solution)/shard_map/ppermute | solution.py:23
  42.5 70.4 %collective-permute-start = (bf16[1,512]{1,0:T(2,128)(2,1)S(1)}, bf16[1,512]{1,0:T(2,128)(2,1)S(1)}, u32[]{:S(2)}, u32[]{:S(2)}) collective-permute-start(bf16[1,512]{1,0:T(2,128)(2,1)S(1)} %bitcast.141), channel_id=1, source_target_pairs={{127,0},{0,1},{1,2},{2,3},{3,4},{4,5},{5,6},{6,7},{7,8},{8,9},{9,1... | collective-permute-start | bytes 3080 | tf_op jit(solution)/shard_map/ppermute | solution.py:23
  46.2 38.1 %collective-permute-start.3 = (bf16[1]{0:T(256)(128)(2,1)}, bf16[1]{0:T(256)(128)(2,1)}, u32[]{:S(2)}, u32[]{:S(2)}) collective-permute-start(bf16[1]{0:T(256)(128)(2,1)} %scatter_fusion.3), channel_id=1, source_target_pairs={{1,0},{2,1},{3,2},{4,3},{5,4},{6,5},{7,6},{8,7},{9,8},{10,9},{11,1... | collective-permute-start | bytes 14 | tf_op jit(solution)/shard_map/ppermute | solution.py:23
  57.0 25.4 %collective-permute-start.2 = (bf16[1]{0:T(256)(128)(2,1)}, bf16[1]{0:T(256)(128)(2,1)}, u32[]{:S(2)}, u32[]{:S(2)}) collective-permute-start(bf16[1]{0:T(256)(128)(2,1)} %scatter_fusion.2), channel_id=1, source_target_pairs={{127,0},{0,1},{1,2},{2,3},{3,4},{4,5},{5,6},{6,7},{7,8},{8,9},{9,1... | collective-permute-start | bytes 14 | tf_op jit(solution)/shard_map/ppermute | solution.py:23
  59.0 10.8 %copy-start.15 = (s32[32]{0:T(128)S(1)}, s32[32]{0:T(128)}, u32[]{:S(2)}) copy-start(s32[32]{0:T(128)} %param.30) | copy-start | bytes 388
  59.0 11.1 %copy-start.14 = (f32[4,512]{1,0:T(4,128)S(1)}, f32[4,512]{1,0:T(4,128)}, u32[]{:S(2)}) copy-start(f32[4,512]{1,0:T(4,128)} %param.31) | copy-start | bytes 24580
  60.7 52.8 %collective-permute-start.5 = (bf16[1,128,128]{2,1,0:T(8,128)(2,1)S(1)}, bf16[1,128,128]{2,1,0:T(8,128)(2,1)S(1)}, u32[]{:S(2)}, u32[]{:S(2)}) collective-permute-start(bf16[1,128,128]{2,1,0:T(8,128)(2,1)S(1)} %bitcast.121), channel_id=1, source_target_pairs={{1,0},{2,1},{3,2},{4,3},{5,4},{6,5},{7,6},{8,7},{9,8},{10,9},{11,1... | collective-permute-start | bytes 98312 | tf_op jit(solution)/shard_map/ppermute | solution.py:23
  70.2 1.7 copy-start.2
  73.7 1.7 copy-start.11
  73.7 4.0 %copy-start.10 = (bf16[32,512]{1,0:T(8,128)(2,1)S(1)}, bf16[32,512]{1,0:T(8,128)(2,1)}, u32[]{:S(2)}) copy-start(bf16[32,512]{1,0:T(8,128)(2,1)} %param.23) | copy-start | bytes 98308
  82.4 16.6 %collective-permute-start.9 = (bf16[1,512]{1,0:T(2,128)(2,1)S(1)}, bf16[1,512]{1,0:T(2,128)(2,1)S(1)}, u32[]{:S(2)}, u32[]{:S(2)}) collective-permute-start(bf16[1,512]{1,0:T(2,128)(2,1)S(1)} %bitcast.143), channel_id=1, source_target_pairs={{1,0},{2,1},{3,2},{4,3},{5,4},{6,5},{7,6},{8,7},{9,8},{10,9},{11,1... | collective-permute-start | bytes 3080 | tf_op jit(solution)/shard_map/ppermute | solution.py:23
  84.3 18.6 %collective-permute-start.8 = (bf16[1,512]{1,0:T(2,128)(2,1)S(1)}, bf16[1,512]{1,0:T(2,128)(2,1)S(1)}, u32[]{:S(2)}, u32[]{:S(2)}) collective-permute-start(bf16[1,512]{1,0:T(2,128)(2,1)S(1)} %bitcast.142), channel_id=1, source_target_pairs={{127,0},{0,1},{1,2},{2,3},{3,4},{4,5},{5,6},{6,7},{7,8},{8,9},{9,1... | collective-permute-start | bytes 3080 | tf_op jit(solution)/shard_map/ppermute | solution.py:23
  90.7 36.6 %all-to-all-start.1 = ((bf16[128,2,512]{2,1,0:T(2,128)(2,1)}), bf16[128,2,512]{2,1,0:T(2,128)(2,1)S(1)}, u32[]{:S(2)}, u32[]{:S(2)}) async-start(bf16[128,2,512]{2,1,0:T(2,128)(2,1)} %scatter_fusion.1), calls=%async_computation.1 | async-start | bytes 524288 | tf_op jit(solution)/shard_map/all_to_all | solution.py:158
  98.5 82.1 %all-reduce.2.cloned.1.call-start = ((), (), s32[]{:S(2)}) async-start(), calls=%async_computation.2 | async-start | bytes 131072 | tf_op jit(solution)/shard_map/psum | solution.py:241
  99.0 14.5 %collective-permute-start.4 = (bf16[1,128,128]{2,1,0:T(8,128)(2,1)S(1)}, bf16[1,128,128]{2,1,0:T(8,128)(2,1)S(1)}, u32[]{:S(2)}, u32[]{:S(2)}) collective-permute-start(bf16[1,128,128]{2,1,0:T(8,128)(2,1)S(1)} %bitcast.122), channel_id=1, source_target_pairs={{127,0},{0,1},{1,2},{2,3},{3,4},{4,5},{5,6},{6,7},{7,8},{8,9},{9,1... | collective-permute-start | bytes 98312 | tf_op jit(solution)/shard_map/ppermute | solution.py:23
  103.0 14.6 %collective-permute-start.7 = (bf16[1,128,128]{2,1,0:T(8,128)(2,1)S(1)}, bf16[1,128,128]{2,1,0:T(8,128)(2,1)S(1)}, u32[]{:S(2)}, u32[]{:S(2)}) collective-permute-start(bf16[1,128,128]{2,1,0:T(8,128)(2,1)S(1)} %bitcast.123), channel_id=1, source_target_pairs={{1,0},{2,1},{3,2},{4,3},{5,4},{6,5},{7,6},{8,7},{9,8},{10,9},{11,1... | collective-permute-start | bytes 98312 | tf_op jit(solution)/shard_map/ppermute | solution.py:23
  110.7 10.4 %collective-permute-start.6 = (bf16[1,128,128]{2,1,0:T(8,128)(2,1)S(1)}, bf16[1,128,128]{2,1,0:T(8,128)(2,1)S(1)}, u32[]{:S(2)}, u32[]{:S(2)}) collective-permute-start(bf16[1,128,128]{2,1,0:T(8,128)(2,1)S(1)} %bitcast.124), channel_id=1, source_target_pairs={{127,0},{0,1},{1,2},{2,3},{3,4},{4,5},{5,6},{6,7},{7,8},{8,9},{9,1... | collective-permute-start | bytes 98312 | tf_op jit(solution)/shard_map/ppermute | solution.py:23
  127.3 0.7 copy-start.16
  127.6 2.3 %copy-start.8 = (bf16[32,512]{1,0:T(8,128)(2,1)}, bf16[32,512]{1,0:T(8,128)(2,1)S(1)}, u32[]{:S(2)}) copy-start(bf16[32,512]{1,0:T(8,128)(2,1)S(1)} %convolution_convert_fusion.2) | copy-start | bytes 98308
  132.4 1.2 copy-start.5
  132.9 1.8 copy-start.9
  134.3 46.3 %copy-start.13 = (f32[512]{0:T(512)S(1)}, f32[512]{0:T(512)}, u32[]{:S(2)}) copy-start(f32[512]{0:T(512)} %param.35) | copy-start | bytes 6148
  134.5 48.2 %copy-start.20 = (f32[512]{0:T(512)S(1)}, f32[512]{0:T(512)}, u32[]{:S(2)}) copy-start(f32[512]{0:T(512)} %param.36) | copy-start | bytes 6148
  142.2 42.2 %copy-start.4 = (bf16[32,128,128]{2,1,0:T(8,128)(2,1)}, bf16[32,128,128]{2,1,0:T(8,128)(2,1)S(1)}, u32[]{:S(2)}) copy-start(bf16[32,128,128]{2,1,0:T(8,128)(2,1)S(1)} %scatter_fusion.9) | copy-start | bytes 3145732
  144.4 40.1 %copy-start.3 = (bf16[32,128,128]{2,1,0:T(8,128)(2,1)}, bf16[32,128,128]{2,1,0:T(8,128)(2,1)S(1)}, u32[]{:S(2)}) copy-start(bf16[32,128,128]{2,1,0:T(8,128)(2,1)S(1)} %scatter_fusion.11) | copy-start | bytes 3145732
  182.7 7.8 %copy-start.7 = (bf16[64,512]{1,0:T(8,128)(2,1)S(1)}, bf16[64,512]{1,0:T(8,128)(2,1)}, u32[]{:S(2)}) copy-start(bf16[64,512]{1,0:T(8,128)(2,1)} %all-reduce.2.cloned.1.call-done) | copy-start | bytes 196612
  182.7 7.9 %copy-start.17 = (f32[512]{0:T(512)S(1)}, f32[512]{0:T(512)}, u32[]{:S(2)}) copy-start(f32[512]{0:T(512)} %param.39) | copy-start | bytes 6148
  190.4 1.2 copy-start.6
  190.4 1.6 copy-start.18
Sparse Core Ops, SparseCore 0:
  135.6 45.0 all-reduce.1
